TPU v7x, 32 devices: a whole 2x2x4 slice. The times are simulated.
32 devices in a mesh: groups: 2 (over x), tiles: 16 (over z, y, core).
Axes of the slice: x: 2, y: 2, z: 4, core: 2. Of those that a mesh axis runs over, the one named last changes fastest.
Arguments:
- coeffs: float32 [8192, 16384], P(('groups', 'tiles')), parts along dimension 0, may hold values from -0.09375 to 0.09375
- occupation: float32 [8192], P(('groups', 'tiles')), parts along dimension 0, may hold values from -1 to 1
- kept_tiles: int32 [64, 2], P('groups'), parts along dimension 0, may hold values from 0 to 255, as said below
- tile_slot: int32 [64], P('groups'), parts along dimension 0, may hold values from 0 to 31, as said below
- blocks: int32 [256, 8], P('groups'), parts along dimension 0, may hold values from 0 to 255, as said below
- batch_slot: int32 [256], P('groups'), parts along dimension 0, may hold values from 0 to 127, as said below
- tables: float32 [256, 512, 256], P(('groups', 'tiles')), parts along dimension 0, may hold values from -3.6 to 3.6
- weights: float32 [256, 256], P(('groups', 'tiles')), parts along dimension 0, may hold values from 0.005 to 0.05
- local_pot: float32 [256, 256], P(('groups', 'tiles')), parts along dimension 0, may hold values from -6 to 6
Outputs:
- density: float32 [256, 256], P(('groups', 'tiles')), parts along dimension 0
- matrix: float32 [64, 4096], P(('groups', 'tiles')), parts along dimension 0
There are 2 independent parts, one for each index of `groups`. A program takes and returns all parts, laid end to end along the dimension named above; each array names one. Nothing has to cross between parts.
Inputs may be any that keep to these rules, and one draw needn't show every extreme that they name: `kept_tiles`: distinct pairs (row block, column block). A permutation; slot tile_slot[k] is held by the device of index tile_slot[k] // 2 along tiles. Of the kept tiles that lie within the blocks of the batches held by one device, at most 2 are held by any one device. Each row names 8 different blocks. The devices come in aligned block clusters of 4 (indices 0 to 3, and so on); all batches held by the devices of one cluster name the same blocks, each batch in an order of its own, and different clusters name disjoint blocks. At most 16 kept tiles lie within the blocks of one batch. A permutation; the tables, weights, potential and density of batch b sit at slot batch_slot[b], held by the device of index batch_slot[b] // 8.
All inputs are finite; a program needn't handle non-finite values.
Results may differ from a plain program's by a relative error of at most 0.0003.
Values sent between devices are 32-bit elements; how exact they have to be, the bound alone decides.
No kernel may reach another device: no remote copies, remote signals or barrier semaphores. Data moves between devices by JAX's collectives and lax.ppermute only.
A program may use at most 128 MiB of HBM per device.

v0:
```python
import jax
import jax.numpy as jnp
from jax import lax
from jax.sharding import PartitionSpec as P

BS = 64
OV = 8


def body(coeffs, occupation, kept_tiles, tile_slot, blocks, batch_slot, tables, weights, local_pot):
    devices = lax.axis_size("tiles")
    my_index = lax.axis_index("tiles")
    kept_count = kept_tiles.shape[0]
    batch_count = tables.shape[0]
    batch_total = batch_slot.shape[0]
    state_count = coeffs.shape[0]
    block_total = coeffs.shape[1] // BS
    points = tables.shape[-1]
    width = OV * BS
    blocked = coeffs.reshape(state_count, block_total, BS)
    left_rows = jnp.take(blocked, kept_tiles[:, 0], axis=1)
    right_rows = jnp.take(blocked, kept_tiles[:, 1], axis=1) * occupation[:, None, None]
    partial = jnp.einsum(
        "srx,sry->rxy", left_rows, right_rows, precision=lax.Precision.HIGHEST
    ).reshape(kept_count, BS * BS)
    tile_values = lax.psum(partial, "tiles")
    ladder_batch = jnp.arange(batch_total, dtype=jnp.int32)
    slot_batch = jnp.zeros((batch_total,), jnp.int32).at[batch_slot].set(ladder_batch)
    my_batches = lax.dynamic_slice_in_dim(slot_batch, my_index * batch_count, batch_count)
    my_blocks = blocks[my_batches]
    canon = jnp.sort(my_blocks[0])
    ladder_ov = jnp.arange(OV, dtype=jnp.int32)
    match = my_blocks[:, :, None] == canon[None, None, :]
    source = jnp.sum(jnp.where(match, ladder_ov[None, :, None], 0), axis=1)
    grid = tables.reshape(batch_count, OV, BS, points)
    canon_tables = jnp.take_along_axis(grid, source[:, :, None, None], axis=1).reshape(
        batch_count, width, points
    )
    row_hit = kept_tiles[:, 0:1] == canon[None, :]
    col_hit = kept_tiles[:, 1:2] == canon[None, :]
    present = jnp.any(row_hit, axis=1) & jnp.any(col_hit, axis=1)
    row_place = jnp.sum(jnp.where(row_hit, ladder_ov[None, :], 0), axis=1)
    col_place = jnp.sum(jnp.where(col_hit, ladder_ov[None, :], 0), axis=1)
    kept_values = jnp.where(present[:, None], tile_values, 0.0).reshape(kept_count, BS, BS)
    dense = (
        jnp.zeros((OV, BS, OV, BS), jnp.float32)
        .at[row_place, :, col_place, :]
        .add(kept_values)
        .reshape(width, width)
    )
    mixed = jnp.einsum("uv,bvp->bup", dense, canon_tables, precision=lax.Precision.HIGH)
    density = jnp.sum(canon_tables * mixed, axis=1)
    potential = local_pot + density - density * density * density / 6.0
    weighted = canon_tables * (weights * potential)[:, None, :]
    full_matrix = jnp.einsum(
        "bup,bvp->uv", weighted, canon_tables, precision=lax.Precision.HIGH
    ).reshape(OV, BS, OV, BS)
    picked = full_matrix[row_place, :, col_place, :].reshape(kept_count, BS * BS)
    contrib = jnp.where(present[:, None], picked, 0.0)
    ladder_kept = jnp.arange(kept_count, dtype=jnp.int32)
    slot_kept = jnp.zeros((kept_count,), jnp.int32).at[tile_slot].set(ladder_kept)
    by_slot = contrib[slot_kept]
    matrix = lax.psum_scatter(by_slot, "tiles", scatter_dimension=0, tiled=True)
    return (density, matrix)


def solution(mesh):
    in_specs = (
        P(("groups", "tiles"), None),
        P(("groups", "tiles")),
        P("groups", None),
        P("groups"),
        P("groups", None),
        P("groups"),
        P(("groups", "tiles"), None, None),
        P(("groups", "tiles"), None),
        P(("groups", "tiles"), None),
    )
    out_specs = (P(("groups", "tiles"), None), P(("groups", "tiles"), None))
    return jax.shard_map(body, mesh=mesh, in_specs=in_specs, out_specs=out_specs, check_vma=False)
```

profile of v0, /device:TPU:1, one launch (start us, length us, event | category | flops | bytes accessed | tf_op | source)
XLA Modules:
  0.0 284.4 jit_solution(15538646823625262167)
XLA Ops:
  7.2 0.0 all-reduce.4.cloned.1.call-start
  7.2 0.8 compare_and_fusion.2
  8.0 17.5 %copy.35 = f32[256,16384]{0,1:T(8,128)} copy(f32[256,16384]{1,0:T(8,128)} %param.11) | data formatting | bytes 33554432 | tf_op args[0]
  25.4 6.4 %gather_fusion.4 = f32[32,256,64]{1,2,0:T(8,128)S(1)} fusion(f32[256,256,64]{0,2,1:T(8,128)} %bitcast.76, s32[1024]{0:T(1024)S(1)} %get-tuple-element.23), kind=kCustom, calls=%fused_computation.clone | custom fusion | bytes 4194432 | tf_op jit(solution)/shard_map/jit(_take)/gather | solution.py:21
  31.9 0.0 copy-start.6
  31.9 7.8 %gather_fusion.5 = f32[32,256,64]{1,2,0:T(8,128)} fusion(f32[256,256,64]{0,2,1:T(8,128)} %bitcast.77, s32[1024]{0:T(1024)S(1)} %get-tuple-element.22), kind=kCustom, calls=%fused_computation.1.clone | custom fusion | bytes 4194432 | tf_op jit(solution)/shard_map/jit(_take)/gather | solution.py:22
  39.7 0.0 copy-start.5
  39.7 0.0 copy-start.7
  39.7 0.0 copy-start.4
  39.7 0.0 copy-start.8
  39.7 0.0 copy-done.6
  39.7 4.0 %fusion.5 = f32[32,64,64]{2,1,0:T(8,128)S(1)} fusion(f32[32,256,64]{1,2,0:T(8,128)} %gather_fusion.5, f32[32,256,64]{1,2,0:T(8,128)S(1)} %gather_fusion.4, f32[256]{0:T(256)S(1)} %copy-done.6, pred[32]{0:T(512)(128)(4,1)S(1)} %get-tuple-element.18, pred[32]{0:T(512)(128)(4,1)S(1)} %get-tuple-element.10), kind=kOutput, calls=%fused_computation.18 | convolution fusion | flops 404226048 | bytes 4719680 | tf_op jit(solution)/shard_map/srx,sry->rxy/dot_general | solution.py:23
  43.7 1.2 reshape.115
  44.9 0.0 all-reduce.4.cloned.1.call-update
  44.9 0.0 all-reduce.6.cloned.1.call-start
  45.0 0.0 copy-done.5
  45.0 0.0 copy-done.7
  45.1 1.0 scatter_custom_fusion
  46.0 0.1 compare_select_fusion.10
  46.1 0.0 copy-done.4
  46.1 0.1 copy.33
  46.2 0.6 gather_fusion
  46.8 1.0 sort.15
  47.8 0.1 compare_reduce_fusion
  47.9 0.1 fusion.22
  47.9 0.1 select_reduce_fusion
  48.1 0.1 reshape.157
  48.1 0.0 copy-done.8
  48.2 0.9 scatter_custom_fusion.2
  49.0 5.0 %gather_fusion.3 = f32[64,64,256]{2,1,0:T(8,128)} fusion(f32[8,8,64,256]{3,2,1,0:T(8,128)} %bitcast.81, s32[64]{0:T(128)S(1)} %reshape.157), kind=kCustom, calls=%fused_computation.5 | custom fusion | bytes 8389120 | tf_op jit(solution)/shard_map/jit(take_along_axis)/gather | solution.py:36
  54.0 4.5 %broadcast_select_fusion = f32[8,8,64,256]{3,2,1,0:T(8,128)} fusion(f32[8,8,64,256]{3,2,1,0:T(8,128)} %bitcast.78, pred[8,8]{1,0:T(8,128)(4,1)S(1)} %compare_and_fusion), kind=kLoop, calls=%fused_computation.22 | loop fusion | flops 1048576 | bytes 8388672 | tf_op jit(solution)/shard_map/jit(take_along_axis)/select_n | solution.py:36
  58.5 5.4 %copy.34 = f32[8,512,256]{1,2,0:T(8,128)} copy(f32[8,512,256]{2,1,0:T(8,128)} %bitcast.79) | data formatting | bytes 8388608 | tf_op jit(solution)/shard_map/jit(take_along_axis)/gather | solution.py:36
  63.9 0.1 broadcast_in_dim.106
  64.0 0.1 broadcast_in_dim.107
  64.1 73.8 %all-reduce.4.cloned.1.call-done = f32[32,4096]{1,0:T(8,128)} async-done(((f32[32,4096]{1,0:T(8,128)}), f32[32,4096]{1,0:T(8,128)}) %all-reduce.4.cloned.1.call-update) | async-done | bytes 524304 | tf_op jit(solution)/shard_map/psum | solution.py:26
  137.9 1.1 broadcast_select_fusion.2
  139.1 0.4 reshape.173
  139.5 0.2 broadcast_in_dim.112
  139.7 2.4 scatter_fusion
  142.1 2.6 copy.36
  144.7 1.9 reshape.196
  146.7 0.0 copy-start.2
  146.7 0.0 copy-start.3
  146.7 0.0 copy-start
  146.7 10.2 %fusion.3 = f32[8,256]{1,0:T(8,128)S(1)} fusion(f32[8,512,256]{1,2,0:T(8,128)} %copy.34, f32[8,512,256]{2,1,0:T(8,128)} %bitcast.80, f32[512,512,1]{1,0,2:T(8,128)S(1)} %reshape.196, pred[8,512]{1,0:T(8,128)(4,1)S(1)} %broadcast_in_dim.107), kind=kOutput, calls=%fused_computation.13 | convolution fusion | flops 3224369152 | bytes 9449472 | tf_op jit(solution)/shard_map/uv,bvp->bup/dot_general | solution.py:51
  156.9 0.0 copy-done.2
  156.9 0.0 copy-done.3
  156.9 0.0 copy-start.1
  157.0 0.0 copy-done
  157.0 3.9 %multiply_bitcast_fusion = (f32[512,8,256]{0,2,1:T(8,128)}, f32[512,8,256]{0,2,1:T(8,128)}) fusion(f32[8,512,256]{1,2,0:T(8,128)S(1)} %copy-done, f32[8,256]{1,0:T(8,128)S(1)} %fusion.20, pred[8,512]{1,0:T(8,128)(4,1)S(1)} %broadcast_in_dim.107), kind=kLoop, calls=%fused_computation.15 | loop fusion | flops 2097152 | bytes 12595200 | tf_op jit(solution)/shard_map/bup,bvp->uv/dot_general | solution.py:55
  160.9 0.0 copy-done.1
  160.9 5.4 %copy.38 = f32[512,8,256]{2,1,0:T(8,128)} copy(f32[512,8,256]{0,2,1:T(8,128)} %get-tuple-element.14) | data formatting | bytes 8388608 | tf_op jit(solution)/shard_map/bup,bvp->uv/dot_general | solution.py:55
  166.4 5.4 %copy.39 = f32[512,8,256]{2,1,0:T(8,128)} copy(f32[512,8,256]{0,2,1:T(8,128)} %get-tuple-element.15) | data formatting | bytes 8388608 | tf_op jit(solution)/shard_map/bup,bvp->uv/dot_general | solution.py:55
  171.8 10.8 %fusion.9 = f32[8,64,8,64]{3,1,2,0:T(8,128)S(1)} fusion(f32[8,64,8,256]{3,2,1,0:T(8,128)} %bitcast.83, f32[8,64,8,256,1]{3,2,1,0,4:T(8,128)} %bitcast.82), kind=kOutput, calls=%fused_computation.23 | convolution fusion | flops 3221225472 | bytes 9437184 | tf_op jit(solution)/shard_map/bup,bvp->uv/dot_general | solution.py:55
  182.6 0.7 gather_fusion.1
  183.3 0.0 copy-start.9
  183.3 0.4 reshape.118
  183.7 0.1 broadcast_select_fusion.1
  183.8 1.5 gather_fusion.2
  185.3 0.0 all-reduce.6.cloned.1.call-update
  185.3 0.0 copy-done.9
  185.3 0.6 dynamic-slice
  186.6 89.5 %all-reduce.6.cloned.1.call-done = f32[32,4096]{1,0:T(8,128)} async-done(((f32[32,4096]{1,0:T(8,128)}), f32[32,4096]{1,0:T(8,128)}) %all-reduce.6.cloned.1.call-update) | async-done | bytes 524304
  276.1 1.5 constant_dynamic-slice_fusion
  (16 shorter events, 0.1 us)
Async XLA Ops:
  7.2 130.8 %all-reduce.4.cloned.1.call-start = ((), (), s32[]{:S(2)}) async-start(), calls=%async_computation | async-start | bytes 1048576 | tf_op jit(solution)/shard_map/psum | solution.py:26
  31.9 7.8 %copy-start.6 = (f32[256]{0:T(256)S(1)}, f32[256]{0:T(256)}, u32[]{:S(2)}) copy-start(f32[256]{0:T(256)} %param.12) | copy-start | bytes 3076
  39.7 5.3 %copy-start.5 = (s32[32,2]{0,1:T(2,128)S(1)}, s32[32,2]{0,1:T(2,128)}, u32[]{:S(2)}) copy-start(s32[32,2]{0,1:T(2,128)} %param.13) | copy-start | bytes 772
  39.7 5.3 %copy-start.7 = (s32[128]{0:T(128)S(1)}, s32[128]{0:T(128)}, u32[]{:S(2)}) copy-start(s32[128]{0:T(128)} %param.16) | copy-start | bytes 1540
  39.7 6.4 %copy-start.4 = (s32[128,8]{0,1:T(8,128)S(1)}, s32[128,8]{0,1:T(8,128)}, u32[]{:S(2)}) copy-start(s32[128,8]{0,1:T(8,128)} %param.15) | copy-start | bytes 12292
  39.7 8.4 %copy-start.8 = (s32[32]{0:T(128)S(1)}, s32[32]{0:T(128)}, u32[]{:S(2)}) copy-start(s32[32]{0:T(128)} %param.14) | copy-start | bytes 388
  44.9 231.1 %all-reduce.6.cloned.1.call-start = ((), (), s32[]{:S(2)}) async-start(), calls=%async_computation.1 | async-start | bytes 1048576
  146.7 10.2 %copy-start.2 = (f32[8,256]{1,0:T(8,128)S(1)}, f32[8,256]{1,0:T(8,128)}, u32[]{:S(2)}) copy-start(f32[8,256]{1,0:T(8,128)} %param.18) | copy-start | bytes 24580
  146.7 10.2 %copy-start.3 = (f32[8,256]{1,0:T(8,128)S(1)}, f32[8,256]{1,0:T(8,128)}, u32[]{:S(2)}) copy-start(f32[8,256]{1,0:T(8,128)} %param.19) | copy-start | bytes 24580
  146.7 10.3 %copy-start = (f32[8,512,256]{1,2,0:T(8,128)S(1)}, f32[8,512,256]{1,2,0:T(8,128)}, u32[]{:S(2)}) copy-start(f32[8,512,256]{1,2,0:T(8,128)} %copy.34) | copy-start | bytes 12582916
  156.9 4.0 %copy-start.1 = (f32[8,256]{1,0:T(8,128)}, f32[8,256]{1,0:T(8,128)S(1)}, u32[]{:S(2)}) copy-start(f32[8,256]{1,0:T(8,128)S(1)} %fusion.3) | copy-start | bytes 24580
  183.3 2.0 copy-start.9
Sparse Core Ops, SparseCore 0:
  45.1 92.8 all-reduce.3
  185.4 90.5 all-reduce.5
where the time goes:
time: 285 us; the launch traced here: 284 us
  waiting for transfers between devices  163 us (57%)
  local copies, waits for them, and re-layouts  66.8 us (23%)
  matrix products  25 us (9%)
  between operations  15 us (5%)
  other arithmetic  14.2 us (5%)
    unnamed x3, waiting for transfers between devices  89.5 us
    psum x1, waiting for transfers between devices, body(): tile_values = lax.psum(partial, 'tiles')  73.8 us
    unnamed x24, local copies, waits for them, and re-layouts  19.7 us
    dot_general x2, local copies, waits for them, and re-layouts, body(): jnp.einsum('bup,bvp->uv', weighted, canon_tables, precision=lax.Precision...  10.9 us
    dot_general x1, matrix products, body(): jnp.einsum('bup,bvp->uv', weighted, canon_tables, precision=lax.Precision...  10.8 us
    gather x3, local copies, waits for them, and re-layouts, body(): jnp.take_along_axis(grid, source[:, :, None, None], axis=1)  10.4 us
    dot_general x1, matrix products, body(): jnp.einsum('uv,bvp->bup', dense, canon_tables, precision=lax.Precision.HIGH)  10.2 us
    gather x1, local copies, waits for them, and re-layouts, body(): jnp.take(blocked, kept_tiles[:, 1], axis=1) * occupation[:, None, None]  7.8 us
  transfers between devices with their start and end apart: 2, of which 2 were waited for; matrix products, arithmetic and copies ran while one was open for 7% of the time, Pallas kernels for 0%

commit v1 on v0

--- a/solution.py
+++ b/solution.py
@@ -23,7 +23,8 @@
     partial = jnp.einsum(
         "srx,sry->rxy", left_rows, right_rows, precision=lax.Precision.HIGHEST
     ).reshape(kept_count, BS * BS)
-    tile_values = lax.psum(partial, "tiles")
+    pieces = lax.all_gather(partial, "tiles", axis=0, tiled=False)
+    tile_values = pieces.sum(axis=0)
     ladder_batch = jnp.arange(batch_total, dtype=jnp.int32)
     slot_batch = jnp.zeros((batch_total,), jnp.int32).at[batch_slot].set(ladder_batch)
     my_batches = lax.dynamic_slice_in_dim(slot_batch, my_index * batch_count, batch_count)

time: 285 us -> 271 us (0.951)
  waiting for transfers between devices: 163 us -> 146 us
  other arithmetic: 14.2 us -> 17.2 us
    psum x1 -> x0, waiting for transfers between devices: 73.8 us -> none  [body(): tile_values = lax.psum(partial, 'tiles')]
    all_gather x0 -> x1, waiting for transfers between devices: none -> 58.6 us  [body(): pieces = lax.all_gather(partial, 'tiles', axis=0, tiled=False)]
    reduce_sum x0 -> x1, other arithmetic: none -> 3.83 us  [body(): tile_values = pieces.sum(axis=0)]
where the time goes in v1:
time: 271 us; the launch traced here: 270 us
  waiting for transfers between devices  146 us (54%)
  local copies, waits for them, and re-layouts  66.5 us (25%)
  matrix products  25 us (9%)
  other arithmetic  17.2 us (6%)
  between operations  15 us (6%)
    unnamed x3, waiting for transfers between devices  87.5 us
    all_gather x1, waiting for transfers between devices, body(): pieces = lax.all_gather(partial, 'tiles', axis=0, tiled=False)  58.6 us
    unnamed x24, local copies, waits for them, and re-layouts  19.7 us
    dot_general x2, local copies, waits for them, and re-layouts, body(): jnp.einsum('bup,bvp->uv', weighted, canon_tables, precision=lax.Precision...  10.9 us
    dot_general x1, matrix products, body(): jnp.einsum('bup,bvp->uv', weighted, canon_tables, precision=lax.Precision...  10.8 us
    gather x3, local copies, waits for them, and re-layouts, body(): jnp.take_along_axis(grid, source[:, :, None, None], axis=1)  10.4 us
    dot_general x1, matrix products, body(): jnp.einsum('uv,bvp->bup', dense, canon_tables, precision=lax.Precision.HIGH)  10.2 us
    gather x1, local copies, waits for them, and re-layouts, body(): jnp.take(blocked, kept_tiles[:, 1], axis=1) * occupation[:, None, None]  7.8 us
  transfers between devices with their start and end apart: 2, of which 2 were waited for; matrix products, arithmetic and copies ran while one was open for 7% of the time, Pallas kernels for 0%

profile of v1, /device:TPU:1, one launch (start us, length us, event | category | flops | bytes accessed | tf_op | source)
XLA Modules:
  0.0 269.8 jit_solution(17676227348851934567)
XLA Ops:
  7.2 0.0 all-gather.2.cloned.1.call-start
  7.2 0.8 compare_and_fusion.2
  8.0 17.5 %copy.35 = f32[256,16384]{0,1:T(8,128)} copy(f32[256,16384]{1,0:T(8,128)} %param.11) | data formatting | bytes 33554432 | tf_op args[0]
  25.4 6.4 %gather_fusion.4 = f32[32,256,64]{1,2,0:T(8,128)S(1)} fusion(f32[256,256,64]{0,2,1:T(8,128)} %bitcast.76, s32[1024]{0:T(1024)S(1)} %get-tuple-element.23), kind=kCustom, calls=%fused_computation.clone | custom fusion | bytes 4194432 | tf_op jit(solution)/shard_map/jit(_take)/gather | solution.py:21
  31.9 0.0 copy-start.6
  31.9 7.8 %gather_fusion.5 = f32[32,256,64]{1,2,0:T(8,128)} fusion(f32[256,256,64]{0,2,1:T(8,128)} %bitcast.77, s32[1024]{0:T(1024)S(1)} %get-tuple-element.22), kind=kCustom, calls=%fused_computation.1.clone | custom fusion | bytes 4194432 | tf_op jit(solution)/shard_map/jit(_take)/gather | solution.py:22
  39.7 0.0 copy-start.4
  39.7 0.0 copy-start.7
  39.7 0.0 copy-done.6
  39.7 3.9 %fusion.5 = f32[32,64,64]{2,1,0:T(8,128)S(1)} fusion(f32[32,256,64]{1,2,0:T(8,128)} %gather_fusion.5, f32[32,256,64]{1,2,0:T(8,128)S(1)} %gather_fusion.4, f32[256]{0:T(256)S(1)} %copy-done.6, pred[32]{0:T(512)(128)(4,1)S(1)} %get-tuple-element.18, pred[32]{0:T(512)(128)(4,1)S(1)} %get-tuple-element.10), kind=kOutput, calls=%fused_computation.18 | convolution fusion | flops 404226048 | bytes 4719680 | tf_op jit(solution)/shard_map/srx,sry->rxy/dot_general | solution.py:23
  43.7 1.2 all_gather_reshape.3
  44.8 0.0 all-gather.2.cloned.1.call-update
  44.9 0.0 all-reduce.3.cloned.1.call-start
  44.9 0.0 copy-done.4
  44.9 0.1 copy.33
  45.0 0.0 copy-done.7
  45.0 1.0 scatter_custom_fusion
  46.0 0.1 compare_select_fusion.10
  46.1 0.6 gather_fusion
  46.7 1.0 sort.15
  47.7 0.1 select_reduce_fusion
  47.8 0.1 reshape.156
  47.8 4.9 %gather_fusion.3 = f32[64,64,256]{2,1,0:T(8,128)} fusion(f32[8,8,64,256]{3,2,1,0:T(8,128)} %bitcast.81, s32[64]{0:T(128)S(1)} %reshape.156), kind=kCustom, calls=%fused_computation.5 | custom fusion | bytes 8389120 | tf_op jit(solution)/shard_map/jit(take_along_axis)/gather | solution.py:37
  52.8 0.0 copy-start.5
  52.8 5.4 %copy.34 = f32[8,512,256]{1,2,0:T(8,128)} copy(f32[8,512,256]{2,1,0:T(8,128)} %bitcast.78) | data formatting | bytes 8388608 | tf_op jit(solution)/shard_map/jit(take_along_axis)/gather | solution.py:37
  58.2 0.1 broadcast_in_dim.110
  58.3 0.1 broadcast_in_dim.111
  58.4 0.0 copy-done.5
  58.4 0.1 compare_reduce_fusion
  58.5 0.0 copy-done.8
  58.5 0.7 scatter_custom_fusion.2
  59.2 0.1 fusion.22
  59.3 4.5 %broadcast_select_fusion = f32[8,8,64,256]{3,2,1,0:T(8,128)} fusion(f32[8,8,64,256]{3,2,1,0:T(8,128)} %bitcast.79, pred[8,8]{1,0:T(8,128)(4,1)S(1)} %compare_and_fusion), kind=kLoop, calls=%fused_computation.22 | loop fusion | flops 1048576 | bytes 8388672 | tf_op jit(solution)/shard_map/jit(take_along_axis)/select_n | solution.py:37
  63.9 58.6 %all-gather.2.cloned.1.call-done = f32[16,32,4096]{2,1,0:T(8,128)} async-done(((f32[1,32,4096]{2,1,0:T(8,128)}), f32[16,32,4096]{2,1,0:T(8,128)}) %all-gather.2.cloned.1.call-update) | async-done | bytes 8388624 | tf_op jit(solution)/shard_map/all_gather | solution.py:26
  122.4 3.8 %reduce_sum.59 = f32[32,4096]{1,0:T(8,128)S(1)} reduce(f32[16,32,4096]{2,1,0:T(8,128)} %all-gather.2.cloned.1.call-done, f32[]{:T(128)} %constant.10.clone.1), dimensions={0}, to_apply=%region_7.9 | reduce | flops 1966080 | bytes 8912900 | tf_op jit(solution)/shard_map/reduce_sum | solution.py:27
  126.3 0.4 reduce_sum.60
  126.7 0.1 broadcast_select_fusion.1
  126.8 0.2 broadcast_in_dim.116
  127.1 2.6 scatter_fusion
  129.7 2.5 copy.36
  132.2 1.9 reshape.195
  134.1 0.0 copy-start.2
  134.2 0.0 copy-start.3
  134.2 0.0 copy-start
  134.2 10.2 %fusion.3 = f32[8,256]{1,0:T(8,128)S(1)} fusion(f32[8,512,256]{1,2,0:T(8,128)} %copy.34, f32[8,512,256]{2,1,0:T(8,128)} %bitcast.80, f32[512,512,1]{1,0,2:T(8,128)S(1)} %reshape.195, pred[8,512]{1,0:T(8,128)(4,1)S(1)} %broadcast_in_dim.111), kind=kOutput, calls=%fused_computation.13 | convolution fusion | flops 3224369152 | bytes 9449472 | tf_op jit(solution)/shard_map/uv,bvp->bup/dot_general | solution.py:52
  144.4 0.0 copy-done.2
  144.4 0.0 copy-done.3
  144.4 0.0 copy-start.1
  144.4 0.0 copy-done
  144.4 3.9 %multiply_bitcast_fusion = (f32[512,8,256]{0,2,1:T(8,128)}, f32[512,8,256]{0,2,1:T(8,128)}) fusion(f32[8,512,256]{1,2,0:T(8,128)S(1)} %copy-done, f32[8,256]{1,0:T(8,128)S(1)} %fusion.20, pred[8,512]{1,0:T(8,128)(4,1)S(1)} %broadcast_in_dim.111), kind=kLoop, calls=%fused_computation.15 | loop fusion | flops 2097152 | bytes 12595200 | tf_op jit(solution)/shard_map/bup,bvp->uv/dot_general | solution.py:56
  148.4 0.0 copy-done.1
  148.4 5.4 %copy.38 = f32[512,8,256]{2,1,0:T(8,128)} copy(f32[512,8,256]{0,2,1:T(8,128)} %get-tuple-element.14) | data formatting | bytes 8388608 | tf_op jit(solution)/shard_map/bup,bvp->uv/dot_general | solution.py:56
  153.8 5.4 %copy.39 = f32[512,8,256]{2,1,0:T(8,128)} copy(f32[512,8,256]{0,2,1:T(8,128)} %get-tuple-element.15) | data formatting | bytes 8388608 | tf_op jit(solution)/shard_map/bup,bvp->uv/dot_general | solution.py:56
  159.3 10.8 %fusion.9 = f32[8,64,8,64]{3,1,2,0:T(8,128)S(1)} fusion(f32[8,64,8,256]{3,2,1,0:T(8,128)} %bitcast.83, f32[8,64,8,256,1]{3,2,1,0,4:T(8,128)} %bitcast.82), kind=kOutput, calls=%fused_computation.23 | convolution fusion | flops 3221225472 | bytes 9437184 | tf_op jit(solution)/shard_map/bup,bvp->uv/dot_general | solution.py:56
  170.1 0.7 gather_fusion.1
  170.8 0.0 copy-start.9
  170.8 0.4 reshape.117
  171.1 0.1 broadcast_select_fusion.2
  171.2 1.5 gather_fusion.2
  172.8 0.0 all-reduce.3.cloned.1.call-update
  172.8 0.0 copy-done.9
  172.8 0.6 dynamic-slice
  174.0 87.4 %all-reduce.3.cloned.1.call-done = f32[32,4096]{1,0:T(8,128)} async-done(((f32[32,4096]{1,0:T(8,128)}), f32[32,4096]{1,0:T(8,128)}) %all-reduce.3.cloned.1.call-update) | async-done | bytes 524304
  261.5 1.5 constant_dynamic-slice_fusion
  (17 shorter events, 0.1 us)
Async XLA Ops:
  7.2 115.3 %all-gather.2.cloned.1.call-start = ((), (), s32[]{:S(2)}) async-start(), calls=%async_computation | async-start | bytes 8912896 | tf_op jit(solution)/shard_map/all_gather | solution.py:26
  31.9 7.8 %copy-start.6 = (f32[256]{0:T(256)S(1)}, f32[256]{0:T(256)}, u32[]{:S(2)}) copy-start(f32[256]{0:T(256)} %param.12) | copy-start | bytes 3076
  39.7 5.2 %copy-start.4 = (s32[128,8]{0,1:T(8,128)S(1)}, s32[128,8]{0,1:T(8,128)}, u32[]{:S(2)}) copy-start(s32[128,8]{0,1:T(8,128)} %param.15) | copy-start | bytes 12292
  39.7 5.3 %copy-start.7 = (s32[128]{0:T(128)S(1)}, s32[128]{0:T(128)}, u32[]{:S(2)}) copy-start(s32[128]{0:T(128)} %param.16) | copy-start | bytes 1540
  44.9 216.6 %all-reduce.3.cloned.1.call-start = ((), (), s32[]{:S(2)}) async-start(), calls=%async_computation.1 | async-start | bytes 1048576
  52.8 5.6 %copy-start.5 = (s32[32,2]{0,1:T(2,128)S(1)}, s32[32,2]{0,1:T(2,128)}, u32[]{:S(2)}) copy-start(s32[32,2]{0,1:T(2,128)} %param.13) | copy-start | bytes 772
  52.8 5.7 %copy-start.8 = (s32[32]{0:T(128)S(1)}, s32[32]{0:T(128)}, u32[]{:S(2)}) copy-start(s32[32]{0:T(128)} %param.14) | copy-start | bytes 388
  134.1 10.2 %copy-start.2 = (f32[8,256]{1,0:T(8,128)S(1)}, f32[8,256]{1,0:T(8,128)}, u32[]{:S(2)}) copy-start(f32[8,256]{1,0:T(8,128)} %param.18) | copy-start | bytes 24580
  134.2 10.2 %copy-start.3 = (f32[8,256]{1,0:T(8,128)S(1)}, f32[8,256]{1,0:T(8,128)}, u32[]{:S(2)}) copy-start(f32[8,256]{1,0:T(8,128)} %param.19) | copy-start | bytes 24580
  134.2 10.3 %copy-start = (f32[8,512,256]{1,2,0:T(8,128)S(1)}, f32[8,512,256]{1,2,0:T(8,128)}, u32[]{:S(2)}) copy-start(f32[8,512,256]{1,2,0:T(8,128)} %copy.34) | copy-start | bytes 12582916
  144.4 4.0 %copy-start.1 = (f32[8,256]{1,0:T(8,128)}, f32[8,256]{1,0:T(8,128)S(1)}, u32[]{:S(2)}) copy-start(f32[8,256]{1,0:T(8,128)S(1)} %fusion.3) | copy-start | bytes 24580
  170.8 2.0 copy-start.9
Sparse Core Ops, SparseCore 0:
  45.0 77.4 all-gather.1
  172.9 88.5 all-reduce.2
